TPU v7x, 32 devices: a whole 2x2x4 slice. The times are simulated.
32 devices in a mesh: row: 8 (over y, x, core), col: 4 (over z).
Axes of the slice: x: 2, y: 2, z: 4, core: 2. Of those that a mesh axis runs over, the one named last changes fastest.
Arguments:
- tokens: bfloat16 [192, 8192], P('col', 'row'), may hold values from -6 to 6
- grad_out: bfloat16 [192, 8192], P('col', 'row'), may hold values from -6 to 6
- gate_weight: bfloat16 [8192, 14336], P('row', 'col'), may hold values from -0.0625 to 0.0625
- up_weight: bfloat16 [8192, 14336], P('row', 'col'), may hold values from -0.0625 to 0.0625
- down_weight: bfloat16 [14336, 8192], P('col', 'row'), may hold values from -0.046875 to 0.046875
Outputs:
- grad_tokens: bfloat16 [192, 8192], P('col', 'row')
- grad_gate_weight: bfloat16 [8192, 14336], P('row', 'col')
- grad_up_weight: bfloat16 [8192, 14336], P('row', 'col')
- grad_down_weight: bfloat16 [14336, 8192], P('col', 'row')
All inputs are finite; a program needn't handle non-finite values.
Results may differ from a plain program's by a relative error of at most 0.024.
Values may be sent and summed in bfloat16 or wider, within the bound.
No kernel may reach another device: no remote copies, remote signals or barrier semaphores. Data moves between devices by JAX's collectives and lax.ppermute only.
A program may use at most 128 MiB of HBM per device.

v0:
```python
import jax
import jax.numpy as jnp
from jax import lax
from jax.sharding import PartitionSpec as P


def contract_first(left, right):
    return lax.dot_general(
        left, right, (((0,), (0,)), ((), ())), preferred_element_type=jnp.float32
    )


def contract_last(left, right):
    return lax.dot_general(
        left, right, (((1,), (1,)), ((), ())), preferred_element_type=jnp.float32
    )


def gated_grads(gate_sum, up_sum, grad_hidden):
    sigmoid_gate = jax.nn.sigmoid(gate_sum)
    hidden = (gate_sum * sigmoid_gate * up_sum).astype(jnp.bfloat16)
    grad_up = (grad_hidden * gate_sum * sigmoid_gate).astype(jnp.bfloat16)
    grad_gate = (
        grad_hidden * up_sum * sigmoid_gate * (1.0 + gate_sum * (1.0 - sigmoid_gate))
    ).astype(jnp.bfloat16)
    return (hidden, grad_gate, grad_up)


def body(tokens, grad_out, gate_weight, up_weight, down_weight):
    tok_all, grad_all = (
        lax.all_gather(tokens, "col", axis=0, tiled=True),
        lax.all_gather(grad_out, "col", axis=0, tiled=True),
    )
    gate_sum, up_sum, grad_hidden = (
        lax.psum(
            jnp.dot(tok_all, gate_weight, preferred_element_type=jnp.float32).astype(jnp.bfloat16),
            "row",
        ).astype(jnp.float32),
        lax.psum(
            jnp.dot(tok_all, up_weight, preferred_element_type=jnp.float32).astype(jnp.bfloat16),
            "row",
        ).astype(jnp.float32),
        lax.psum(contract_last(grad_all, down_weight).astype(jnp.bfloat16), "row").astype(
            jnp.float32
        ),
    )
    hidden, grad_gate, grad_up = gated_grads(gate_sum, up_sum, grad_hidden)
    acc_gate = contract_first(tok_all, grad_gate)
    acc_up = contract_first(tok_all, grad_up)
    acc_down = contract_first(hidden, grad_all)
    partial_grad = contract_last(grad_gate, gate_weight) + contract_last(grad_up, up_weight)
    grad_tokens = lax.psum_scatter(
        partial_grad.astype(jnp.bfloat16), "col", scatter_dimension=0, tiled=True
    )
    return (
        grad_tokens,
        acc_gate.astype(jnp.bfloat16),
        acc_up.astype(jnp.bfloat16),
        acc_down.astype(jnp.bfloat16),
    )


def solution(mesh):
    return jax.shard_map(
        body,
        mesh=mesh,
        in_specs=(
            P("col", "row"),
            P("col", "row"),
            P("row", "col"),
            P("row", "col"),
            P("col", "row"),
        ),
        out_specs=(P("col", "row"), P("row", "col"), P("row", "col"), P("col", "row")),
        check_vma=False,
    )
```

profile of v0, /device:TPU:0, one launch (start us, length us, event | category | flops | bytes accessed | tf_op | source)
XLA Modules:
  0.0 188.0 jit_solution(11670191383653160460)
XLA Ops:
  7.2 0.0 all-reduce.3.cloned.1.call-start
  7.2 16.5 %all_gather.7 = bf16[192,1024]{1,0:T(8,128)(2,1)S(1)} all-gather(bf16[48,1024]{1,0:T(8,128)(2,1)} %param.5), channel_id=1, replica_groups=mesh['row'=8,'col'=4] {'col'}, dimensions={0}, use_global_device_ids=true | all-gather | bytes 491520 | tf_op jit(solution)/shard_map/all_gather | solution.py:31
  23.7 15.8 %all_gather.6 = bf16[192,1024]{1,0:T(8,128)(2,1)S(1)} all-gather(bf16[48,1024]{1,0:T(8,128)(2,1)} %param.6), channel_id=1, replica_groups=mesh['row'=8,'col'=4] {'col'}, dimensions={0}, use_global_device_ids=true | all-gather | bytes 491520 | tf_op jit(solution)/shard_map/all_gather | solution.py:32
  39.4 0.0 copy-start.4
  39.4 0.0 slice-start
  39.4 5.9 %convolution_convert_fusion.4 = bf16[192,3584]{1,0:T(8,128)(2,1)} fusion(bf16[192,1024]{1,0:T(8,128)(2,1)S(1)} %all_gather.7, bf16[1024,3584]{1,0:T(8,128)(2,1)} %param.8), kind=kOutput, calls=%fused_computation.6 | convolution fusion | flops 1409974272 | bytes 9109504 | tf_op jit(solution)/shard_map/dot_general | solution.py:40
  45.4 0.0 copy-done.4
  45.4 0.0 slice-start.1
  45.4 2.7 %convolution_convert_fusion.3 = bf16[192,3584]{1,0:T(8,128)(2,1)} fusion(bf16[192,1024]{1,0:T(8,128)(2,1)S(1)} %all_gather.7, bf16[1024,3584]{1,0:T(8,128)(2,1)S(1)} %copy-done.4), kind=kOutput, calls=%fused_computation.5 | convolution fusion | flops 1409974272 | bytes 9109504 | tf_op jit(solution)/shard_map/dot_general | solution.py:36
  48.1 0.0 slice-done
  48.1 0.0 slice-done.1
  48.1 3.6 %convolution_convert_fusion.5 = bf16[192,3584]{1,0:T(8,128)(2,1)} fusion(bf16[192,1024]{1,0:T(8,128)(2,1)S(1)} %all_gather.6, bf16[3584,1024]{1,0:T(8,128)(2,1)S(1)} %bitcast.18), kind=kOutput, calls=%fused_computation.7 | convolution fusion | flops 1409974272 | bytes 9109504 | tf_op jit(solution)/shard_map/dot_general | solution.py:14
  51.7 0.0 all-reduce.3.cloned.1.call-update
  51.7 0.2 reduce-scatter.2.cloned.1.call-start
  51.9 81.2 %all-reduce.3.cloned.1.call-done = (bf16[192,3584]{1,0:T(8,128)(2,1)}, bf16[192,3584]{1,0:T(8,128)(2,1)}, bf16[192,3584]{1,0:T(8,128)(2,1)}) async-done(((bf16[192,3584]{1,0:T(8,128)(2,1)}, bf16[192,3584]{1,0:T(8,128)(2,1)}, bf16[192,3584]{1,0:T(8,128)(2,1)}), (bf16[192,3584]{1,0:T(8,128)(2,1)}, bf16[192,3584]{1,0:T(8,128)(2,1)}, bf16[192,3584]{1,0:T(8,128)(2,1)})) %all-reduce.3.cloned.1.call-update) | async-done | bytes 4128784 | tf_op jit(solution)/shard_map/psum | solution.py:39
  133.2 7.0 %fusion.1 = bf16[1024,3584]{0,1:T(8,128)(2,1)} fusion(bf16[192,1024]{1,0:T(8,128)(2,1)S(1)} %all_gather.7, bf16[192,3584]{1,0:T(8,128)(2,1)} %get-tuple-element.10, bf16[192,3584]{1,0:T(8,128)(2,1)} %get-tuple-element.9), kind=kOutput, calls=%fused_computation.4 | convolution fusion | flops 1418461184 | bytes 10485760 | tf_op jit(solution)/shard_map/dot_general | solution.py:8
  140.2 0.0 copy-done
  140.2 0.0 copy-done.1
  140.2 0.0 copy-done.3
  140.2 0.0 slice-start.2
  140.3 1.2 fusion.4
  141.5 0.0 slice-start.3
  141.5 5.7 %fusion.18 = f32[192,1024]{1,0:T(8,128)S(1)} fusion(bf16[192,3584]{1,0:T(8,128)(2,1)S(1)} %fusion.4, bf16[1024,3584]{1,0:T(8,128)(2,1)} %param.7), kind=kOutput, calls=%fused_computation.28 | convolution fusion | flops 1409286144 | bytes 9502720 | tf_op jit(solution)/shard_map/dot_general | solution.py:14
  147.2 0.0 slice-done.2
  147.3 0.0 slice-done.3
  147.3 3.4 %fusion.14 = bf16[192,1024]{1,0:T(8,128)(2,1)} fusion(f32[192,1024]{1,0:T(8,128)S(1)} %fusion.18, bf16[1024,3584]{1,0:T(8,128)(2,1)S(1)} %bitcast.20, bf16[192,3584]{1,0:T(8,128)(2,1)S(1)} %copy-done.1, bf16[192,3584]{1,0:T(8,128)(2,1)S(1)} %copy-done.3), kind=kOutput, calls=%fused_computation.26 | convolution fusion | flops 1415184384 | bytes 11272192 | tf_op jit(solution)/shard_map/dot_general | solution.py:14
  150.6 0.0 reduce-scatter.2.cloned.1.call-update
  150.7 5.2 %fusion = bf16[1024,3584]{0,1:T(8,128)(2,1)} fusion(bf16[192,3584]{1,0:T(8,128)(2,1)S(1)} %fusion.4, bf16[192,1024]{1,0:T(8,128)(2,1)S(1)} %all_gather.7), kind=kOutput, calls=%fused_computation.3 | convolution fusion | flops 1412956160 | bytes 9109504 | tf_op jit(solution)/shard_map/dot_general | solution.py:8
  155.8 10.0 %copy.9 = bf16[1024,3584]{1,0:T(8,128)(2,1)} copy(bf16[1024,3584]{0,1:T(8,128)(2,1)} %fusion) | data formatting | bytes 14680064
  165.8 10.0 %copy.10 = bf16[1024,3584]{1,0:T(8,128)(2,1)} copy(bf16[1024,3584]{0,1:T(8,128)(2,1)} %fusion.1) | data formatting | bytes 14680064
  175.8 0.0 copy-done.2
  175.8 5.3 %convolution_convert_fusion = bf16[3584,1024]{1,0:T(8,128)(2,1)} fusion(bf16[192,1024]{1,0:T(8,128)(2,1)S(1)} %all_gather.6, bf16[192,3584]{1,0:T(8,128)(2,1)S(1)} %copy-done, bf16[192,3584]{1,0:T(8,128)(2,1)S(1)} %copy-done.2), kind=kOutput, calls=%fused_computation | convolution fusion | flops 1418461184 | bytes 10485760 | tf_op jit(solution)/shard_map/dot_general | solution.py:8
  (7 shorter events, 0.0 us)
Async XLA Ops:
  7.2 126.0 %all-reduce.3.cloned.1.call-start = ((), (), s32[]{:S(2)}) async-start(), calls=%async_computation.2 | async-start | bytes 8257536 | tf_op jit(solution)/shard_map/psum | solution.py:39
  39.4 5.9 %copy-start.4 = (bf16[1024,3584]{1,0:T(8,128)(2,1)S(1)}, bf16[1024,3584]{1,0:T(8,128)(2,1)}, u32[]{:S(2)}) copy-start(bf16[1024,3584]{1,0:T(8,128)(2,1)} %param.7) | copy-start | bytes 22020100
  39.4 8.6 %slice-start = ((s8[7340032]{0:T(1024)(128)(4,1)}), s8[4194304]{0:T(1024)(128)(4,1)S(1)}, s32[]{:S(2)}) async-start(s8[7340032]{0:T(1024)(128)(4,1)} %bitcast.17), calls=%async_computation.3 | async-start | bytes 8388608
  45.4 2.7 %slice-start.1 = ((s8[7340032]{0:T(1024)(128)(4,1)}), s8[3145728]{0:T(1024)(128)(4,1)S(1)}, s32[]{:S(2)}) async-start(s8[7340032]{0:T(1024)(128)(4,1)} %bitcast.17), calls=%async_computation.4 | async-start | bytes 6291456
  51.7 129.4 %reduce-scatter.2.cloned.1.call-start = ((), (), s32[]{:S(2)}) async-start(), calls=%async_computation.1 | async-start | bytes 491520 | tf_op jit(solution)/shard_map/reduce_scatter | solution.py:52
  133.2 7.1 %copy-start = (bf16[192,3584]{1,0:T(8,128)(2,1)S(1)}, bf16[192,3584]{1,0:T(8,128)(2,1)}, u32[]{:S(2)}) copy-start(bf16[192,3584]{1,0:T(8,128)(2,1)} %get-tuple-element.8) | copy-start | bytes 4128772
  133.2 7.1 %copy-start.1 = (bf16[192,3584]{1,0:T(8,128)(2,1)S(1)}, bf16[192,3584]{1,0:T(8,128)(2,1)}, u32[]{:S(2)}) copy-start(bf16[192,3584]{1,0:T(8,128)(2,1)} %get-tuple-element.10) | copy-start | bytes 4128772
  133.2 7.1 %copy-start.3 = (bf16[192,3584]{1,0:T(8,128)(2,1)S(1)}, bf16[192,3584]{1,0:T(8,128)(2,1)}, u32[]{:S(2)}) copy-start(bf16[192,3584]{1,0:T(8,128)(2,1)} %get-tuple-element.9) | copy-start | bytes 4128772
  140.2 7.0 %slice-start.2 = ((s8[7340032]{0:T(1024)(128)(4,1)}), s8[4194304]{0:T(1024)(128)(4,1)S(1)}, s32[]{:S(2)}) async-start(s8[7340032]{0:T(1024)(128)(4,1)} %bitcast.19), calls=%async_computation.5 | async-start | bytes 8388608
  141.5 5.8 %slice-start.3 = ((s8[7340032]{0:T(1024)(128)(4,1)}), s8[3145728]{0:T(1024)(128)(4,1)S(1)}, s32[]{:S(2)}) async-start(s8[7340032]{0:T(1024)(128)(4,1)} %bitcast.19), calls=%async_computation.6 | async-start | bytes 6291456
  165.8 10.0 %copy-start.2 = (bf16[192,3584]{1,0:T(8,128)(2,1)S(1)}, bf16[192,3584]{1,0:T(8,128)(2,1)}, u32[]{:S(2)}) copy-start(bf16[192,3584]{1,0:T(8,128)(2,1)} %get-tuple-element.10) | copy-start | bytes 4128772
Sparse Core Ops, SparseCore 0:
  51.8 81.3 all-reduce.2
  150.8 20.8 reduce-scatter.1
where the time goes:
time: 189 us; the launch traced here: 188 us
  waiting for transfers between devices  81.3 us (43%)
  matrix products  38.8 us (21%)
  blocking collectives  32.2 us (17%)
  local copies, waits for them, and re-layouts  20.1 us (11%)
  between operations  14.1 us (7%)
    psum x1, waiting for transfers between devices, body(): lax.psum(jnp.dot(tok_all, up_weight, preferred_element_type=jnp.float32)....  81.2 us
    unnamed x20, local copies, waits for them, and re-layouts  20.1 us
    dot_general x3, matrix products, contract_first(): lax.dot_general(left, right, (((0,), (0,)), ((), ())), preferred_element_...  17.5 us
    all_gather x1, blocking collectives, body(): lax.all_gather(tokens, 'col', axis=0, tiled=True)  16.5 us
    all_gather x1, blocking collectives, body(): lax.all_gather(grad_out, 'col', axis=0, tiled=True)  15.8 us
    dot_general x3, matrix products, contract_last(): lax.dot_general(left, right, (((1,), (1,)), ((), ())), preferred_element_...  12.7 us
    dot_general x1, matrix products, body(): jnp.dot(tok_all, up_weight, preferred_element_type=jnp.float32)  5.91 us
  transfers between devices with their start and end apart: 2, of which 1 were waited for; matrix products, arithmetic and copies ran while one was open for 16% of the time, Pallas kernels for 0%

commit v1 on v0

--- a/solution.py
+++ b/solution.py
@@ -36,9 +36,14 @@
             jnp.dot(tok_all, gate_weight, preferred_element_type=jnp.float32).astype(jnp.bfloat16),
             "row",
         ).astype(jnp.float32),
-        lax.psum(
-            jnp.dot(tok_all, up_weight, preferred_element_type=jnp.float32).astype(jnp.bfloat16),
-            "row",
+        jnp.sum(
+            lax.all_gather(
+                jnp.dot(tok_all, up_weight, preferred_element_type=jnp.float32).astype(
+                    jnp.bfloat16
+                ),
+                "row",
+            ),
+            axis=0,
         ).astype(jnp.float32),
         lax.psum(contract_last(grad_all, down_weight).astype(jnp.bfloat16), "row").astype(
             jnp.float32

time: 189 us -> 233 us (1.23)
  waiting for transfers between devices: 81.3 us -> 112 us
  other arithmetic: 1.21 us -> 9.37 us
  matrix products: 38.8 us -> 44.9 us
    all_gather x0 -> x1, waiting for transfers between devices: none -> 50.4 us  [body(): lax.all_gather(jnp.dot(tok_all, up_weight, preferred_element_type=jnp.flo...]
    psum x1, waiting for transfers between devices: 81.2 us -> 60.9 us  [body(): lax.psum(contract_last(grad_all, down_weight).astype(jnp.bfloat16), 'row')]
    reduce_sum x0 -> x1, other arithmetic: none -> 6.42 us  [body(): jnp.sum(lax.all_gather(jnp.dot(tok_all, up_weight, preferred_element_type...]
    dot_general x1, matrix products: 2.7 us -> 5.91 us  [body(): jnp.dot(tok_all, gate_weight, preferred_element_type=jnp.float32)]
    dot_general x3, matrix products: 12.7 us -> 15.8 us  [contract_last(): lax.dot_general(left, right, (((1,), (1,)), ((), ())), preferred_element_...]
    unnamed x20 -> x12, local copies, waits for them, and re-layouts: 20.1 us -> 20.3 us
  transfers between devices with their start and end apart: 2 -> 3, of which waited for: 1 -> 3; matrix products, arithmetic and copies ran while one was open for 16% -> 19% of each run, Pallas kernels for 0% -> 0%
where the time goes in v1:
time: 233 us
  waiting for transfers between devices  112 us (48%)
  matrix products  44.9 us (19%)
  blocking collectives  32.4 us (14%)
  local copies, waits for them, and re-layouts  20.3 us (9%)
  between operations  13.8 us (6%)
  other arithmetic  9.37 us (4%)
    psum x1, waiting for transfers between devices, body(): lax.psum(contract_last(grad_all, down_weight).astype(jnp.bfloat16), 'row')  60.9 us
    all_gather x1, waiting for transfers between devices, body(): lax.all_gather(jnp.dot(tok_all, up_weight, preferred_element_type=jnp.flo...  50.4 us
    unnamed x12, local copies, waits for them, and re-layouts  20.3 us
    dot_general x3, matrix products, contract_first(): lax.dot_general(left, right, (((0,), (0,)), ((), ())), preferred_element_...  17.5 us
    all_gather x1, blocking collectives, body(): lax.all_gather(tokens, 'col', axis=0, tiled=True)  16.5 us
    all_gather x1, blocking collectives, body(): lax.all_gather(grad_out, 'col', axis=0, tiled=True)  15.9 us
    dot_general x3, matrix products, contract_last(): lax.dot_general(left, right, (((1,), (1,)), ((), ())), preferred_element_...  15.8 us
    reduce_sum x1, other arithmetic, body(): jnp.sum(lax.all_gather(jnp.dot(tok_all, up_weight, preferred_element_type...  6.42 us
  transfers between devices with their start and end apart: 3, of which 3 were waited for; matrix products, arithmetic and copies ran while one was open for 19% of the time, Pallas kernels for 0%

profile of v1, /device:TPU:0, one launch (start us, length us, event | category | flops | bytes accessed | tf_op | source)
XLA Modules:
  0.0 232.7 jit_solution(14774838372785459877)
XLA Ops:
  7.2 0.0 all-reduce.3.cloned.1.call-start
  7.2 16.5 %all_gather.13 = bf16[192,1024]{1,0:T(8,128)(2,1)S(1)} all-gather(bf16[48,1024]{1,0:T(8,128)(2,1)} %param.5), channel_id=1, replica_groups=mesh['row'=8,'col'=4] {'col'}, dimensions={0}, use_global_device_ids=true | all-gather | bytes 491520 | tf_op jit(solution)/shard_map/all_gather | solution.py:31
  23.7 15.9 %all_gather.12 = bf16[192,1024]{1,0:T(8,128)(2,1)S(1)} all-gather(bf16[48,1024]{1,0:T(8,128)(2,1)} %param.6), channel_id=1, replica_groups=mesh['row'=8,'col'=4] {'col'}, dimensions={0}, use_global_device_ids=true | all-gather | bytes 491520 | tf_op jit(solution)/shard_map/all_gather | solution.py:32
  39.6 0.0 slice-start.1
  39.6 5.9 %convolution_convert_fusion.3 = bf16[192,3584]{1,0:T(8,128)(2,1)} fusion(bf16[192,1024]{1,0:T(8,128)(2,1)S(1)} %all_gather.13, bf16[1024,3584]{1,0:T(8,128)(2,1)} %param.7), kind=kOutput, calls=%fused_computation.5 | convolution fusion | flops 1409974272 | bytes 9109504 | tf_op jit(solution)/shard_map/dot_general | solution.py:36
  45.5 0.0 slice-done
  45.5 0.0 slice-done.1
  45.5 3.6 %convolution_convert_fusion.5 = bf16[192,3584]{1,0:T(8,128)(2,1)} fusion(bf16[192,1024]{1,0:T(8,128)(2,1)S(1)} %all_gather.12, bf16[3584,1024]{1,0:T(8,128)(2,1)S(1)} %bitcast.20), kind=kOutput, calls=%fused_computation.7 | convolution fusion | flops 1409974272 | bytes 9109504 | tf_op jit(solution)/shard_map/dot_general | solution.py:14
  49.1 0.0 all-reduce.3.cloned.1.call-update
  49.1 0.0 all-gather.3.cloned.1.call-start
  49.2 5.8 %convolution_convert_fusion.4 = bf16[192,3584]{1,0:T(8,128)(2,1)} fusion(bf16[192,1024]{1,0:T(8,128)(2,1)S(1)} %all_gather.13, bf16[1024,3584]{1,0:T(8,128)(2,1)} %param.8), kind=kOutput, calls=%fused_computation.6 | convolution fusion | flops 1409974272 | bytes 9109504 | tf_op jit(solution)/shard_map/dot_general | solution.py:41
  55.0 0.0 all-gather.3.cloned.1.call-update
  55.0 0.0 reduce-scatter.2.cloned.1.call-start
  55.0 60.9 %all-reduce.3.cloned.1.call-done = (bf16[192,3584]{1,0:T(8,128)(2,1)}, bf16[192,3584]{1,0:T(8,128)(2,1)}) async-done(((bf16[192,3584]{1,0:T(8,128)(2,1)}, bf16[192,3584]{1,0:T(8,128)(2,1)}), (bf16[192,3584]{1,0:T(8,128)(2,1)}, bf16[192,3584]{1,0:T(8,128)(2,1)})) %all-reduce.3.cloned.1.call-update) | async-done | bytes 2752528 | tf_op jit(solution)/shard_map/psum | solution.py:48
  116.0 7.0 %fusion.1 = bf16[1024,3584]{0,1:T(8,128)(2,1)} fusion(bf16[192,1024]{1,0:T(8,128)(2,1)S(1)} %all_gather.13, bf16[192,3584]{1,0:T(8,128)(2,1)} %get-tuple-element.9, bf16[192,3584]{1,0:T(8,128)(2,1)} %get-tuple-element.8), kind=kOutput, calls=%fused_computation.4 | convolution fusion | flops 1418461184 | bytes 10485760 | tf_op jit(solution)/shard_map/dot_general | solution.py:8
  123.0 10.2 %copy.10 = bf16[1024,3584]{1,0:T(8,128)(2,1)} copy(bf16[1024,3584]{0,1:T(8,128)(2,1)} %fusion.1) | data formatting | bytes 14680064
  133.2 50.4 %all-gather.3.cloned.1.call-done = bf16[1536,3584]{1,0:T(8,128)(2,1)} async-done(((bf16[192,3584]{1,0:T(8,128)(2,1)}), bf16[1536,3584]{1,0:T(8,128)(2,1)}) %all-gather.3.cloned.1.call-update) | async-done | bytes 11010064 | tf_op jit(solution)/shard_map/all_gather | solution.py:40
  183.6 6.4 %reduce_sum.12 = bf16[192,3584]{1,0:T(8,128)(2,1)S(1)} reduce(bf16[8,192,3584]{2,1,0:T(8,128)(2,1)} %bitcast.18, bf16[]{:T(256)} %constant.1.clone.1), dimensions={0}, to_apply=%region_1.0 | reduce | flops 4816896 | bytes 12386306 | tf_op jit(solution)/shard_map/reduce_sum | solution.py:39
  190.0 3.0 %fusion.4 = bf16[192,3584]{1,0:T(8,128)(2,1)S(1)} fusion(bf16[192,3584]{1,0:T(8,128)(2,1)S(1)} %reduce_sum.12, bf16[192,3584]{1,0:T(8,128)(2,1)} %get-tuple-element.8, bf16[192,3584]{1,0:T(8,128)(2,1)} %get-tuple-element.9), kind=kLoop, calls=%fused_computation.16 | loop fusion | flops 8945664 | bytes 5505024 | tf_op jit(solution)/shard_map/convert_element_type | solution.py:25
  192.9 0.0 copy-start
  193.0 0.0 copy-start.2
  193.0 5.7 %fusion.18 = f32[192,1024]{1,0:T(8,128)S(1)} fusion(bf16[192,3584]{1,0:T(8,128)(2,1)S(1)} %fusion.4, bf16[1024,3584]{1,0:T(8,128)(2,1)} %param.7), kind=kOutput, calls=%fused_computation.28 | convolution fusion | flops 1409286144 | bytes 9502720 | tf_op jit(solution)/shard_map/dot_general | solution.py:14
  198.7 0.0 copy-done
  198.7 0.0 copy-done.2
  198.7 6.4 %fusion.14 = bf16[192,1024]{1,0:T(8,128)(2,1)} fusion(f32[192,1024]{1,0:T(8,128)S(1)} %fusion.18, bf16[1024,3584]{1,0:T(8,128)(2,1)} %param.8, bf16[192,3584]{1,0:T(8,128)(2,1)S(1)} %copy-done, bf16[192,3584]{1,0:T(8,128)(2,1)S(1)} %copy-done.2), kind=kOutput, calls=%fused_computation.26 | convolution fusion | flops 1415184384 | bytes 11272192 | tf_op jit(solution)/shard_map/dot_general | solution.py:14
  205.2 0.0 reduce-scatter.2.cloned.1.call-update
  205.2 5.2 %fusion = bf16[1024,3584]{0,1:T(8,128)(2,1)} fusion(bf16[192,3584]{1,0:T(8,128)(2,1)S(1)} %fusion.4, bf16[192,1024]{1,0:T(8,128)(2,1)S(1)} %all_gather.13), kind=kOutput, calls=%fused_computation.3 | convolution fusion | flops 1412956160 | bytes 9109504 | tf_op jit(solution)/shard_map/dot_general | solution.py:8
  210.4 0.0 copy-start.1
  210.4 10.1 %copy.9 = bf16[1024,3584]{1,0:T(8,128)(2,1)} copy(bf16[1024,3584]{0,1:T(8,128)(2,1)} %fusion) | data formatting | bytes 14680064
  220.5 0.0 copy-done.1
  220.5 5.3 %convolution_convert_fusion = bf16[3584,1024]{1,0:T(8,128)(2,1)} fusion(bf16[192,1024]{1,0:T(8,128)(2,1)S(1)} %all_gather.12, bf16[192,3584]{1,0:T(8,128)(2,1)S(1)} %reduce_sum.12, bf16[192,3584]{1,0:T(8,128)(2,1)S(1)} %copy-done.1), kind=kOutput, calls=%fused_computation | convolution fusion | flops 1418461184 | bytes 10485760 | tf_op jit(solution)/shard_map/dot_general | solution.py:8
  225.7 0.4 reduce-scatter.2.cloned.1.call-done
  (2 shorter events, 0.0 us)
Async XLA Ops:
  7.2 108.8 %all-reduce.3.cloned.1.call-start = ((), (), s32[]{:S(2)}) async-start(), calls=%async_computation.3 | async-start | bytes 5505024 | tf_op jit(solution)/shard_map/psum | solution.py:48
  23.7 21.8 %slice-start = ((s8[7340032]{0:T(1024)(128)(4,1)}), s8[4194304]{0:T(1024)(128)(4,1)S(1)}, s32[]{:S(2)}) async-start(s8[7340032]{0:T(1024)(128)(4,1)} %bitcast.19), calls=%async_computation.4 | async-start | bytes 8388608
  39.6 5.9 %slice-start.1 = ((s8[7340032]{0:T(1024)(128)(4,1)}), s8[3145728]{0:T(1024)(128)(4,1)S(1)}, s32[]{:S(2)}) async-start(s8[7340032]{0:T(1024)(128)(4,1)} %bitcast.19), calls=%async_computation.5 | async-start | bytes 6291456
  49.1 134.4 %all-gather.3.cloned.1.call-start = ((), (), s32[]{:S(2)}) async-start(), calls=%async_computation.2 | async-start | bytes 12386304 | tf_op jit(solution)/shard_map/all_gather | solution.py:40
  55.0 171.2 %reduce-scatter.2.cloned.1.call-start = ((), (), s32[]{:S(2)}) async-start(), calls=%async_computation.1 | async-start | bytes 491520 | tf_op jit(solution)/shard_map/reduce_scatter | solution.py:57
  192.9 5.8 %copy-start = (bf16[192,3584]{1,0:T(8,128)(2,1)S(1)}, bf16[192,3584]{1,0:T(8,128)(2,1)}, u32[]{:S(2)}) copy-start(bf16[192,3584]{1,0:T(8,128)(2,1)} %get-tuple-element.9) | copy-start | bytes 4128772
  193.0 5.8 %copy-start.2 = (bf16[192,3584]{1,0:T(8,128)(2,1)S(1)}, bf16[192,3584]{1,0:T(8,128)(2,1)}, u32[]{:S(2)}) copy-start(bf16[192,3584]{1,0:T(8,128)(2,1)} %get-tuple-element.8) | copy-start | bytes 4128772
  210.4 10.1 %copy-start.1 = (bf16[192,3584]{1,0:T(8,128)(2,1)S(1)}, bf16[192,3584]{1,0:T(8,128)(2,1)}, u32[]{:S(2)}) copy-start(bf16[192,3584]{1,0:T(8,128)(2,1)} %get-tuple-element.9) | copy-start | bytes 4128772
Sparse Core Ops, SparseCore 0:
  49.3 66.6 all-reduce.2
  118.4 65.0 all-gather.2
  205.3 20.8 reduce-scatter.1
